TPU v7x, 256 devices: a whole 4x4x8 slice. The times are simulated.
256 devices in a mesh: dp: 4 (over x_lo, core), expert: 64 (over z, y, x_hi).
Axes of the slice: x: 4 (x_hi: 2, x_lo: 2; x = x_hi * 2 + x_lo), y: 4, z: 8, core: 2. Of those that a mesh axis runs over, the one named last changes fastest.
Arguments:
- prev_acts: bfloat16 [4, 64, 128, 3584], P('dp', 'expert'), may hold values from -6 to 6
- prev_cot: bfloat16 [4, 64, 128, 512], P('dp', 'expert'), may hold values from -0.59765625 to 0.59765625
- weights: bfloat16 [64, 3584, 512], P('expert', 'dp'), may hold values from -0.09375 to 0.09375
- first_moment: float32 [64, 3584, 512], P('expert', 'dp'), may hold values from -1.8 to 1.8
- second_moment: float32 [64, 3584, 512], P('expert', 'dp'), may hold values from 0.1 to 2
- tokens: bfloat16 [4, 64, 128, 3584], P('dp', 'expert'), may hold values from -6 to 6
- routing: int32 [4, 64, 128, 2], P('dp', 'expert'), may hold values from 0 to 15, all different within a row; in each aligned block of 128 rows (0 to 127, 128 to 255, ..., all dimensions but the last counted through in order) at most 24 rows name the same one
- gates: bfloat16 [4, 64, 128, 2], P('dp', 'expert'), may hold values from 0.19921875 to 1
- token_counts: int32 [4, 64], P('dp', 'expert'), may hold values from 64 to 128
- old_owner: int32 [16], replicated, may hold values from 0 to 15, each once
- new_owner: int32 [16], replicated, may hold values from 0 to 15, each once
Outputs:
- expert_hidden: bfloat16 [4, 64, 1536, 256], P('dp', 'expert')
- new_weights: bfloat16 [64, 3584, 512], P('expert', 'dp')
- new_first: float32 [64, 3584, 512], P('expert', 'dp')
- new_second: float32 [64, 3584, 512], P('expert', 'dp')
Inputs may be any that keep to these rules, and one draw needn't show every extreme that they name: `routing`: each token names 2 different hot experts; within the rows of one device no hot expert is named by more than 24 rows. `old_owner`: each is a permutation of the 16 groups. `new_owner`: each is a permutation of the 16 groups.
All inputs are finite; a program needn't handle non-finite values.
Results may differ from a plain program's by a relative error of at most 0.013.
Values may be sent and summed in bfloat16 or wider, within the bound.
No kernel may reach another device: no remote copies, remote signals or barrier semaphores. Data moves between devices by JAX's collectives and lax.ppermute only.
A program may use at most 128 MiB of HBM per device.

v0:
```python
import jax
import jax.numpy as jnp
from jax import lax
from jax.sharding import Mesh
from jax.sharding import PartitionSpec as P

D = 3584
GRP = 4
SCALE_PAD = 128
beta_first = 0.9
beta_second = 0.95
learning = 0.00022
decay_rate = 0.1
epsilon = 1e-08
first_fix = 1.0 - 0.9**40
second_fix = 1.0 - 0.95**40


def adamw(weight_now, first_now, second_now, gradient):
    first_next = beta_first * first_now + (1.0 - beta_first) * gradient
    second_next = beta_second * second_now + (1.0 - beta_second) * gradient * gradient
    stepped = weight_now.astype(jnp.float32) * (1.0 - learning * decay_rate) - learning * (
        first_next / first_fix
    ) / (jnp.sqrt(second_next / second_fix) + epsilon)
    return (stepped.astype(jnp.bfloat16), first_next, second_next)


def migrate(state, group_source, groups, mode=None):
    layers, rows_dev, width = state.shape
    piece_rows = rows_dev // groups
    split = state.reshape(layers, groups, piece_rows, width)
    spread = lax.all_to_all(split, "grp", split_axis=1, concat_axis=1, tiled=True)
    chosen = jnp.take(spread, group_source, axis=1, mode=mode)
    home = lax.all_to_all(chosen, "grp", split_axis=1, concat_axis=1, tiled=True)
    return home.reshape(layers, rows_dev, width)


def pack_tokens(token_block, route_block, gate_block, limit, hot_index, capacity):
    valid = jnp.arange(token_block.shape[0], dtype=jnp.int32) < limit
    hits = (route_block[:, :, None] == hot_index[None, None, :]) & valid[:, None, None]
    named = jnp.sum(hits.astype(jnp.int32), axis=1)
    scales = jnp.sum(jnp.where(hits, gate_block.astype(jnp.float32)[:, :, None], 0.0), axis=1)
    ranks = jnp.cumsum(named, axis=0) - named
    slots = jnp.arange(capacity, dtype=jnp.int32)
    placed = (ranks.T[:, None, :] == slots[None, :, None]) & (named.T[:, None, :] == 1)
    packed = jnp.einsum(
        "hct,td->hcd", placed.astype(jnp.bfloat16), token_block, preferred_element_type=jnp.float32
    ).astype(jnp.bfloat16)
    gate_scale = jnp.einsum("hct,th->hc", placed.astype(jnp.float32), scales).astype(jnp.bfloat16)
    return (packed, gate_scale)


def local(
    prev_acts,
    prev_cot,
    weights,
    first_moment,
    second_moment,
    tokens,
    routing,
    gates,
    token_counts,
    old_owner,
    new_owner,
):
    groups = lax.axis_size("grp")
    experts = groups * GRP
    token_slots = tokens.shape[2]
    capacity = min(token_slots, 3 * token_slots // groups)
    width = weights.shape[2]
    hidden_units = width // 2
    activations = prev_acts[0, 0]
    cotangent = prev_cot[0, 0]
    hot_index = jnp.arange(groups, dtype=jnp.int32)
    holder = jnp.sum(
        jnp.where(new_owner[None, :] == hot_index[:, None], hot_index[None, :], 0), axis=1
    )
    group_source = jnp.take(old_owner, holder)
    packed, gate_scale = pack_tokens(
        tokens[0, 0], routing[0, 0], gates[0, 0], token_counts[0, 0], holder, capacity
    )
    scale_cols = jnp.zeros((groups, capacity, SCALE_PAD), jnp.bfloat16).at[:, :, 0].set(gate_scale)
    payload = jnp.concatenate([packed, scale_cols], axis=2)
    by_group = lax.all_to_all(payload, "grp", split_axis=0, concat_axis=0, tiled=True)
    grads = lax.psum_scatter(
        lax.dot_general(
            activations, cotangent, (((0,), (0,)), ((), ())), preferred_element_type=jnp.float32
        ).astype(jnp.bfloat16),
        "dp",
        scatter_dimension=0,
        tiled=True,
    )
    by_group, grads = lax.optimization_barrier((by_group, grads))
    grads = grads.astype(jnp.float32)
    near = lax.all_gather(by_group, "ylo", axis=0, tiled=False)
    near = near.reshape(2 * groups * capacity, D + SCALE_PAD)
    stepped, first_next, second_next = adamw(weights[0], first_moment[0], second_moment[0], grads)
    weight_home = migrate(stepped[None], group_source, groups)
    new_weight = weight_home[0]
    moments = jnp.stack([first_next.astype(jnp.bfloat16), second_next.astype(jnp.bfloat16)])
    moments, new_weight = lax.optimization_barrier((moments, new_weight))
    moved = migrate(moments, group_source, groups, mode="clip")
    both = lax.all_gather(new_weight, ("xhi", "dp"), axis=0, tiled=True)
    both = both.reshape(2, -1, width)
    both = jnp.pad(both, ((0, 0), (0, SCALE_PAD), (0, 0)))
    projected = jnp.stack(
        [jnp.dot(near, both[k], preferred_element_type=jnp.float32) for k in range(2)]
    )
    scaling = near[:, D].astype(jnp.float32)
    result = (
        jax.nn.silu(projected[:, :, :hidden_units])
        * projected[:, :, hidden_units:]
        * scaling[None, :, None]
    ).astype(jnp.bfloat16)
    xhi = lax.axis_index("xhi")
    own = lax.dynamic_index_in_dim(result, xhi, axis=0, keepdims=False)
    other = lax.dynamic_index_in_dim(result, 1 - xhi, axis=0, keepdims=False)
    for_partner = lax.ppermute(other, "xhi", perm=[(0, 1), (1, 0)])
    mine = jnp.where(
        xhi == 0, jnp.stack([own, for_partner]), jnp.stack([for_partner, own])
    ).reshape(2, 2, groups, capacity, hidden_units)
    hidden = jnp.transpose(mine, (2, 1, 0, 3, 4)).reshape(1, 1, experts * capacity, hidden_units)
    return (
        hidden,
        weight_home,
        moved[0].astype(jnp.float32)[None],
        moved[1].astype(jnp.float32)[None],
    )


def solution(mesh):
    n_dp = mesh.shape["dp"]
    n_expert = mesh.shape["expert"]
    mesh4 = Mesh(mesh.devices.reshape(n_dp, n_expert // GRP, 2, 2), ("dp", "grp", "ylo", "xhi"))
    ex = ("grp", "ylo", "xhi")
    in_specs = (
        P("dp", ex, None, None),
        P("dp", ex, None, None),
        P(ex, "dp", None),
        P(ex, "dp", None),
        P(ex, "dp", None),
        P("dp", ex, None, None),
        P("dp", ex, None, None),
        P("dp", ex, None, None),
        P("dp", ex),
        P(),
        P(),
    )
    out_specs = (P("dp", ex, None, None), P(ex, "dp", None), P(ex, "dp", None), P(ex, "dp", None))
    return jax.shard_map(local, mesh=mesh4, in_specs=in_specs, out_specs=out_specs, check_vma=False)
```

profile of v0, /device:TPU:6, one launch (start us, length us, event | category | flops | bytes accessed | tf_op | source)
XLA Modules:
  0.0 284.6 jit_solution(10818399610023016619)
XLA Ops:
  7.2 1.1 copy-done
  8.3 3.8 %convolution_convert_fusion = bf16[3584,512]{1,0:T(8,128)(2,1)} fusion(bf16[1,1,128,3584]{3,2,1,0:T(8,128)(2,1)S(1)} %copy-done, bf16[1,1,128,512]{3,2,1,0:T(8,128)(2,1)} %param.14), kind=kOutput, calls=%fused_computation.5 | convolution fusion | flops 471597056 | bytes 4718592 | tf_op jit(solution)/shard_map/dot_general | solution.py:86
  12.2 0.0 all-gather.6.cloned.1.call-start
  12.3 0.6 copy-done.9
  12.8 0.1 select_reduce_fusion.1
  13.6 0.1 convert_reduce_fusion
  13.7 0.1 copy.42
  13.8 0.2 reduce_window_sum.11
  14.0 0.1 copy.44
  14.1 0.1 select_reduce_fusion
  14.2 0.2 fusion.30
  14.3 0.2 copy.45
  14.5 0.9 convolution_convert_fusion.1
  15.4 0.2 fusion.7
  15.6 80.3 %all_to_all.25 = bf16[16,24,3712]{2,1,0:T(8,128)(2,1)} all-to-all(bf16[16,24,3712]{2,1,0:T(8,128)(2,1)S(1)} %fusion.7), channel_id=1, replica_groups=mesh['dp'=4,'grp'=16,'ylo'=2,'xhi'=2] {'grp'}, dimensions={0} | all-to-all | bytes 5701632 | tf_op jit(solution)/shard_map/all_to_all | solution.py:84
  96.0 1.1 copy-done.5
  97.1 5.1 %fusion.10 = (bf16[896,512]{1,0:T(8,128)(2,1)}, bf16[1,896,512]{2,1,0:T(8,128)(2,1)S(1)}, bf16[1,896,512]{2,1,0:T(8,128)(2,1)}) fusion(bf16[1,896,512]{2,1,0:T(8,128)(2,1)S(1)} %copy-done.5, bf16[896,512]{1,0:T(8,128)(2,1)} %reduce-scatter.2.cloned.1.call-done, f32[1,896,512]{2,1,0:T(8,128)} %param.16, f32[1,896,512]{2,1,0:T(8,128)} %param.17), kind=kLoop, calls=%fused_computation.22 | loop fusion | flops 8257536 | bytes 8257536 | tf_op jit(solution)/shard_map/convert_element_type | solution.py:25
  102.3 3.8 %all-to-all-start.1 = ((bf16[1,16,56,512]{3,2,0,1:T(8,128)(2,1)}), bf16[1,16,56,512]{3,2,0,1:T(8,128)(2,1)S(1)}, u32[]{:S(2)}, u32[]{:S(2)}) async-start(bf16[1,16,56,512]{3,2,0,1:T(8,128)(2,1)} %bitcast.125), calls=%async_computation.2 | async-start | bytes 1835008 | tf_op jit(solution)/shard_map/all_to_all | solution.py:32
  106.1 0.7 gather_fusion
  106.8 24.6 %all-to-all-done.1 = bf16[1,16,56,512]{3,2,0,1:T(8,128)(2,1)S(1)} async-done(((bf16[1,16,56,512]{3,2,0,1:T(8,128)(2,1)}), bf16[1,16,56,512]{3,2,0,1:T(8,128)(2,1)S(1)}, u32[]{:S(2)}, u32[]{:S(2)}) %all-to-all-start.1) | async-done | bytes 917536 | tf_op jit(solution)/shard_map/all_to_all | solution.py:32
  131.4 1.5 gather_fusion.1
  132.9 2.2 fusion.26
  135.2 3.8 %all-to-all-start.2 = ((bf16[1,16,56,512]{3,2,0,1:T(8,128)(2,1)}), bf16[1,16,56,512]{3,2,0,1:T(8,128)(2,1)S(1)}, u32[]{:S(2)}, u32[]{:S(2)}) async-start(bf16[1,16,56,512]{3,2,0,1:T(8,128)(2,1)} %fusion.26), calls=%async_computation.3 | async-start | bytes 1835008 | tf_op jit(solution)/shard_map/all_to_all | solution.py:34
  139.0 0.0 all-gather.4.cloned.1.call-start
  139.0 2.6 pad_maximum_fusion
  141.6 24.7 %all-to-all-done.2 = bf16[1,16,56,512]{3,2,0,1:T(8,128)(2,1)S(1)} async-done(((bf16[1,16,56,512]{3,2,0,1:T(8,128)(2,1)}), bf16[1,16,56,512]{3,2,0,1:T(8,128)(2,1)S(1)}, u32[]{:S(2)}, u32[]{:S(2)}) %all-to-all-start.2) | async-done | bytes 917536 | tf_op jit(solution)/shard_map/all_to_all | solution.py:34
  166.4 0.9 copy-done.2
  167.3 3.0 %copy.50 = bf16[2,16,56,512]{3,2,0,1:T(8,128)(2,1)} copy(bf16[2,16,56,512]{3,2,1,0:T(8,128)(2,1)} %bitcast.120) | data formatting | bytes 3670016 | tf_op jit(solution)/shard_map/reshape | solution.py:31
  170.3 3.7 %all-to-all-start.3 = ((bf16[2,16,56,512]{3,2,0,1:T(8,128)(2,1)}), bf16[2,16,56,512]{3,2,0,1:T(8,128)(2,1)S(1)}, u32[]{:S(2)}, u32[]{:S(2)}) async-start(bf16[2,16,56,512]{3,2,0,1:T(8,128)(2,1)} %copy.50), calls=%async_computation.4 | async-start | bytes 3670016 | tf_op jit(solution)/shard_map/all_to_all | solution.py:32
  174.0 45.9 %all-to-all-done.3 = bf16[2,16,56,512]{3,2,0,1:T(8,128)(2,1)S(1)} async-done(((bf16[2,16,56,512]{3,2,0,1:T(8,128)(2,1)}), bf16[2,16,56,512]{3,2,0,1:T(8,128)(2,1)S(1)}, u32[]{:S(2)}, u32[]{:S(2)}) %all-to-all-start.3) | async-done | bytes 1835040 | tf_op jit(solution)/shard_map/all_to_all | solution.py:32
  219.9 1.9 gather_fusion.2
  221.7 3.7 %all-to-all-start.4 = ((bf16[2,16,56,512]{3,2,0,1:T(8,128)(2,1)}), bf16[2,16,56,512]{3,2,0,1:T(8,128)(2,1)S(1)}, u32[]{:S(2)}, u32[]{:S(2)}) async-start(bf16[2,16,56,512]{3,2,0,1:T(8,128)(2,1)} %bitcast.121), calls=%async_computation.5 | async-start | bytes 3670016 | tf_op jit(solution)/shard_map/all_to_all | solution.py:34
  225.5 0.9 slice.57
  226.5 0.1 copy.53
  226.6 14.0 %all-gather.4.cloned.1.call-done = bf16[7168,512]{1,0:T(8,128)(2,1)} async-done(((bf16[896,512]{1,0:T(8,128)(2,1)}), bf16[7168,512]{1,0:T(8,128)(2,1)}) %all-gather.4.cloned.1.call-update) | async-done | bytes 7340048 | tf_op jit(solution)/shard_map/all_gather | solution.py:103
  240.6 6.3 %fusion.15 = f32[1,768,512]{2,1,0:T(8,128)S(1)} fusion(bf16[768,3712]{1,0:T(8,128)(2,1)} %bitcast.131, bf16[2,3584,512]{2,1,0:T(8,128)(2,1)} %bitcast.135), kind=kOutput, calls=%fused_computation.28 | convolution fusion | flops 2919235584 | bytes 14614528 | tf_op jit(solution)/shard_map/dot_general | solution.py:107
  247.0 1.2 copy-done.8
  248.1 3.1 %fusion.18 = f32[1,768,512]{2,1,0:T(8,128)S(1)} fusion(bf16[768,3712]{1,0:T(8,128)(2,1)S(1)} %bitcast.132, bf16[2,3584,512]{2,1,0:T(8,128)(2,1)S(1)} %bitcast.136), kind=kOutput, calls=%fused_computation.29 | convolution fusion | flops 2919235584 | bytes 14614528 | tf_op jit(solution)/shard_map/dot_general | solution.py:107
  251.2 0.4 fusion.14
  251.6 0.1 constant_dynamic-slice_fusion
  251.7 2.5 collective-permute-start
  254.3 17.5 %all-to-all-done.4 = bf16[2,16,56,512]{3,2,0,1:T(8,128)(2,1)S(1)} async-done(((bf16[2,16,56,512]{3,2,0,1:T(8,128)(2,1)}), bf16[2,16,56,512]{3,2,0,1:T(8,128)(2,1)S(1)}, u32[]{:S(2)}, u32[]{:S(2)}) %all-to-all-start.4) | async-done | bytes 1835040 | tf_op jit(solution)/shard_map/all_to_all | solution.py:34
  271.8 0.1 fusion.43
  271.9 1.5 convert.5
  273.4 1.5 convert.6
  274.9 1.3 fusion.28
  276.2 1.0 copy.49
  277.1 0.9 copy.56
  (36 shorter events, 0.3 us)
Async XLA Ops:
  7.2 1.2 copy-start
  7.2 88.7 %reduce-scatter.2.cloned.1.call-start = ((), (), s32[]{:S(2)}) async-start(), calls=%async_computation.6 | async-start | bytes 4587520 | tf_op jit(solution)/shard_map/reduce_scatter | solution.py:85
  12.2 0.7 copy-start.9
  12.2 1.4 copy-start.7
  12.2 1.9 copy-start.10
  12.2 2.3 copy-start.4
  12.2 213.3 %all-gather.6.cloned.1.call-start = ((), (), s32[]{:S(2)}) async-start(), calls=%async_computation.8 | async-start | bytes 8552448 | tf_op jit(solution)/shard_map/all_gather | solution.py:95
  95.9 1.2 copy-start.5
  102.2 3.8 %copy-start.1 = (s32[16]{0:T(128)S(1)}, s32[16]{0:T(128)}, u32[]{:S(2)}) copy-start(s32[16]{0:T(128)} %param.22) | copy-start | bytes 196
  102.3 29.1 %all-to-all-start.1 = ((bf16[1,16,56,512]{3,2,0,1:T(8,128)(2,1)}), bf16[1,16,56,512]{3,2,0,1:T(8,128)(2,1)S(1)}, u32[]{:S(2)}, u32[]{:S(2)}) async-start(bf16[1,16,56,512]{3,2,0,1:T(8,128)(2,1)} %bitcast.125), calls=%async_computation.2 | async-start | bytes 1835008 | tf_op jit(solution)/shard_map/all_to_all | solution.py:32
  135.2 31.2 %all-to-all-start.2 = ((bf16[1,16,56,512]{3,2,0,1:T(8,128)(2,1)}), bf16[1,16,56,512]{3,2,0,1:T(8,128)(2,1)S(1)}, u32[]{:S(2)}, u32[]{:S(2)}) async-start(bf16[1,16,56,512]{3,2,0,1:T(8,128)(2,1)} %fusion.26), calls=%async_computation.3 | async-start | bytes 1835008 | tf_op jit(solution)/shard_map/all_to_all | solution.py:34
  139.0 101.6 %all-gather.4.cloned.1.call-start = ((), (), s32[]{:S(2)}) async-start(), calls=%async_computation.7 | async-start | bytes 8257536 | tf_op jit(solution)/shard_map/all_gather | solution.py:103
  166.4 0.9 copy-start.2
  170.3 49.6 %all-to-all-start.3 = ((bf16[2,16,56,512]{3,2,0,1:T(8,128)(2,1)}), bf16[2,16,56,512]{3,2,0,1:T(8,128)(2,1)S(1)}, u32[]{:S(2)}, u32[]{:S(2)}) async-start(bf16[2,16,56,512]{3,2,0,1:T(8,128)(2,1)} %copy.50), calls=%async_computation.4 | async-start | bytes 3670016 | tf_op jit(solution)/shard_map/all_to_all | solution.py:32
  221.7 50.0 %all-to-all-start.4 = ((bf16[2,16,56,512]{3,2,0,1:T(8,128)(2,1)}), bf16[2,16,56,512]{3,2,0,1:T(8,128)(2,1)S(1)}, u32[]{:S(2)}, u32[]{:S(2)}) async-start(bf16[2,16,56,512]{3,2,0,1:T(8,128)(2,1)} %bitcast.121), calls=%async_computation.5 | async-start | bytes 3670016 | tf_op jit(solution)/shard_map/all_to_all | solution.py:34
  240.6 6.3 %copy-start.6 = (bf16[32,24,3712]{2,1,0:T(8,128)(2,1)S(1)}, bf16[32,24,3712]{2,1,0:T(8,128)(2,1)}, u32[]{:S(2)}) copy-start(bf16[32,24,3712]{2,1,0:T(8,128)(2,1)} %all-gather.6.cloned.1.call-done) | copy-start | bytes 17104900
  240.6 7.5 %copy-start.8 = (bf16[7168,512]{1,0:T(8,128)(2,1)S(1)}, bf16[7168,512]{1,0:T(8,128)(2,1)}, u32[]{:S(2)}) copy-start(bf16[7168,512]{1,0:T(8,128)(2,1)} %all-gather.4.cloned.1.call-done) | copy-start | bytes 22020100
  251.7 23.1 %collective-permute-start = (bf16[768,256]{1,0:T(8,128)(2,1)S(1)}, bf16[768,256]{1,0:T(8,128)(2,1)}, u32[]{:S(2)}, u32[]{:S(2)}) collective-permute-start(bf16[768,256]{1,0:T(8,128)(2,1)S(1)} %get-tuple-element.30), channel_id=1, source_target_pairs={{0,1},{1,0},{2,3},{3,2},{4,5},{5,4},{6,7},{7,6},{8,9},{9,8},{10,11... | collective-permute-start | bytes 1179656 | tf_op jit(solution)/shard_map/ppermute | solution.py:118
  274.8 2.3 copy-start.3
Sparse Core Ops, SparseCore 0:
  12.3 45.8 reduce-scatter.1
  96.1 95.5 all-gather.5
  194.1 46.5 all-gather.3
where the time goes:
time: 285 us
  waiting for transfers between devices  127 us (45%)
  blocking collectives  80.3 us (28%)
  starting transfers between devices  17.7 us (6%)
  local copies, waits for them, and re-layouts  15.5 us (5%)
  other arithmetic  15.4 us (5%)
  between operations  14.6 us (5%)
  matrix products  14.2 us (5%)
    all_to_all x1, blocking collectives, local(): lax.all_to_all(payload, 'grp', split_axis=0, concat_axis=0, tiled=True)  80.3 us
    all_to_all x2, waiting for transfers between devices, migrate(): lax.all_to_all(split, 'grp', split_axis=1, concat_axis=1, tiled=True)  70.5 us
    all_to_all x2, waiting for transfers between devices, migrate(): lax.all_to_all(chosen, 'grp', split_axis=1, concat_axis=1, tiled=True)  42.2 us
    all_gather x1, waiting for transfers between devices, local(): both = lax.all_gather(new_weight, ('xhi', 'dp'), axis=0, tiled=True)  14 us
    dot_general x2, matrix products, local(): jnp.dot(near, both[k], preferred_element_type=jnp.float32)  9.38 us
    all_to_all x2, starting transfers between devices, migrate(): lax.all_to_all(chosen, 'grp', split_axis=1, concat_axis=1, tiled=True)  7.54 us
    all_to_all x2, starting transfers between devices, migrate(): lax.all_to_all(split, 'grp', split_axis=1, concat_axis=1, tiled=True)  7.49 us
    unnamed x24, local copies, waits for them, and re-layouts  6 us
  transfers between devices with their start and end apart: 8, of which 5 were waited for; matrix products, arithmetic and copies ran while one was open for 12% of the time, Pallas kernels for 0%

commit v1 on v0

--- a/solution.py
+++ b/solution.py
@@ -31,7 +31,10 @@
     split = state.reshape(layers, groups, piece_rows, width)
     spread = lax.all_to_all(split, "grp", split_axis=1, concat_axis=1, tiled=True)
     chosen = jnp.take(spread, group_source, axis=1, mode=mode)
-    home = lax.all_to_all(chosen, "grp", split_axis=1, concat_axis=1, tiled=True)
+    home = jnp.concatenate(
+        lax.all_to_all(jnp.stack(jnp.split(chosen, lax.axis_size("grp"), axis=1)), "grp", 0, 0),
+        axis=1,
+    )
     return home.reshape(layers, rows_dev, width)
 
 

time: 285 us -> 311 us (1.091)
  local copies, waits for them, and re-layouts: 15.5 us -> 42.2 us
    unnamed x24 -> x56, local copies, waits for them, and re-layouts: 6 us -> 31.4 us
    all_to_all x2, waiting for transfers between devices: 42.2 us -> 57 us  [migrate(): lax.all_to_all(jnp.stack(jnp.split(chosen, lax.axis_size('grp'), axis=1))...]
    all_gather x1, waiting for transfers between devices: 14 us -> 0.02 us  [local(): both = lax.all_gather(new_weight, ('xhi', 'dp'), axis=0, tiled=True)]
  transfers between devices with their start and end apart: 8 -> 8, of which waited for: 5 -> 4; matrix products, arithmetic and copies ran while one was open for 12% -> 18% of each run, Pallas kernels for 0% -> 0%
where the time goes in v1:
time: 311 us; the launch traced here: 310 us
  waiting for transfers between devices  128 us (41%)
  blocking collectives  80.4 us (26%)
  local copies, waits for them, and re-layouts  42.2 us (14%)
  starting transfers between devices  16.7 us (5%)
  between operations  14.7 us (5%)
  other arithmetic  14.5 us (5%)
  matrix products  14.2 us (5%)
    all_to_all x1, blocking collectives, local(): lax.all_to_all(payload, 'grp', split_axis=0, concat_axis=0, tiled=True)  80.4 us
    all_to_all x2, waiting for transfers between devices, migrate(): lax.all_to_all(split, 'grp', split_axis=1, concat_axis=1, tiled=True)  70.6 us
    all_to_all x2, waiting for transfers between devices, migrate(): lax.all_to_all(jnp.stack(jnp.split(chosen, lax.axis_size('grp'), axis=1))...  57 us
    unnamed x56, local copies, waits for them, and re-layouts  31.4 us
    dot_general x2, matrix products, local(): jnp.dot(near, both[k], preferred_element_type=jnp.float32)  9.39 us
    all_to_all x2, starting transfers between devices, migrate(): lax.all_to_all(jnp.stack(jnp.split(chosen, lax.axis_size('grp'), axis=1))...  7.59 us
    all_to_all x2, starting transfers between devices, migrate(): lax.all_to_all(split, 'grp', split_axis=1, concat_axis=1, tiled=True)  7.48 us
  transfers between devices with their start and end apart: 8, of which 4 were waited for; matrix products, arithmetic and copies ran while one was open for 18% of the time, Pallas kernels for 0%

profile of v1, /device:TPU:6, one launch (start us, length us, event | category | flops | bytes accessed | tf_op | source)
XLA Modules:
  0.0 310.5 jit_solution(4107325109135792310)
XLA Ops:
  7.2 1.1 copy-done
  8.3 3.8 %convolution_convert_fusion = bf16[3584,512]{1,0:T(8,128)(2,1)} fusion(bf16[1,1,128,3584]{3,2,1,0:T(8,128)(2,1)S(1)} %copy-done, bf16[1,1,128,512]{3,2,1,0:T(8,128)(2,1)} %param.14), kind=kOutput, calls=%fused_computation.5 | convolution fusion | flops 471597056 | bytes 4718592 | tf_op jit(solution)/shard_map/dot_general | solution.py:89
  14.5 0.9 convolution_convert_fusion.1
  15.6 80.4 %all_to_all.25 = bf16[16,24,3712]{2,1,0:T(8,128)(2,1)} all-to-all(bf16[16,24,3712]{2,1,0:T(8,128)(2,1)S(1)} %fusion.7), channel_id=1, replica_groups=mesh['dp'=4,'grp'=16,'ylo'=2,'xhi'=2] {'grp'}, dimensions={0} | all-to-all | bytes 5701632 | tf_op jit(solution)/shard_map/all_to_all | solution.py:87
  96.1 5.1 %fusion.10 = (bf16[896,512]{1,0:T(8,128)(2,1)}, bf16[1,896,512]{2,1,0:T(8,128)(2,1)S(1)}, bf16[1,896,512]{2,1,0:T(8,128)(2,1)}) fusion(bf16[1,896,512]{2,1,0:T(8,128)(2,1)S(1)} %copy-done.6, bf16[896,512]{1,0:T(8,128)(2,1)} %reduce-scatter.2.cloned.1.call-done, f32[1,896,512]{2,1,0:T(8,128)} %param.16, f32[1,896,512]{2,1,0:T(8,128)} %param.17), kind=kLoop, calls=%fused_computation.22 | loop fusion | flops 8257536 | bytes 8257536 | tf_op jit(solution)/shard_map/convert_element_type | solution.py:25
  101.2 3.8 %all-to-all-start.1 = ((bf16[1,16,56,512]{3,2,0,1:T(8,128)(2,1)}), bf16[1,16,56,512]{3,2,0,1:T(8,128)(2,1)S(1)}, u32[]{:S(2)}, u32[]{:S(2)}) async-start(bf16[1,16,56,512]{3,2,0,1:T(8,128)(2,1)} %bitcast.266), calls=%async_computation.2 | async-start | bytes 1835008 | tf_op jit(solution)/shard_map/all_to_all | solution.py:32
  105.1 0.7 gather_fusion
  105.8 24.6 %all-to-all-done.1 = bf16[1,16,56,512]{3,2,0,1:T(8,128)(2,1)S(1)} async-done(((bf16[1,16,56,512]{3,2,0,1:T(8,128)(2,1)}), bf16[1,16,56,512]{3,2,0,1:T(8,128)(2,1)S(1)}, u32[]{:S(2)}, u32[]{:S(2)}) %all-to-all-start.1) | async-done | bytes 917536 | tf_op jit(solution)/shard_map/all_to_all | solution.py:32
  130.4 1.5 gather_fusion.1
  131.9 1.3 bitcast_select_fusion
  133.2 0.6 constant_dynamic-update-slice_fusion.15
  134.5 0.6 constant_dynamic-update-slice_fusion.13
  143.3 3.9 %all-to-all-start.2 = ((bf16[16,1,1,56,512]{4,3,2,1,0:T(8,128)(2,1)}), bf16[16,1,1,56,512]{4,3,2,1,0:T(8,128)(2,1)S(1)}, u32[]{:S(2)}, u32[]{:S(2)}) async-start(bf16[16,1,1,56,512]{4,3,2,1,0:T(8,128)(2,1)} %constant_dynamic-update-slice_fusion), calls=%async_computation.3 | async-start | bytes 1835008 | tf_op jit(solution)/shard_map/all_to_all | solution.py:35
  147.2 2.6 pad_maximum_fusion
  149.8 24.5 %all-to-all-done.2 = bf16[16,1,1,56,512]{4,3,2,1,0:T(8,128)(2,1)S(1)} async-done(((bf16[16,1,1,56,512]{4,3,2,1,0:T(8,128)(2,1)}), bf16[16,1,1,56,512]{4,3,2,1,0:T(8,128)(2,1)S(1)}, u32[]{:S(2)}, u32[]{:S(2)}) %all-to-all-start.2) | async-done | bytes 917536 | tf_op jit(solution)/shard_map/all_to_all | solution.py:35
  174.3 0.9 copy-done.2
  175.2 3.0 copy.48
  178.2 3.7 %all-to-all-start.3 = ((bf16[2,16,56,512]{3,2,0,1:T(8,128)(2,1)}), bf16[2,16,56,512]{3,2,0,1:T(8,128)(2,1)S(1)}, u32[]{:S(2)}, u32[]{:S(2)}) async-start(bf16[2,16,56,512]{3,2,0,1:T(8,128)(2,1)} %copy.48), calls=%async_computation.4 | async-start | bytes 3670016 | tf_op jit(solution)/shard_map/all_to_all | solution.py:32
  181.9 46.0 %all-to-all-done.3 = bf16[2,16,56,512]{3,2,0,1:T(8,128)(2,1)S(1)} async-done(((bf16[2,16,56,512]{3,2,0,1:T(8,128)(2,1)}), bf16[2,16,56,512]{3,2,0,1:T(8,128)(2,1)S(1)}, u32[]{:S(2)}, u32[]{:S(2)}) %all-to-all-start.3) | async-done | bytes 1835040 | tf_op jit(solution)/shard_map/all_to_all | solution.py:32
  227.9 1.9 gather_fusion.2
  229.8 1.7 fusion.48
  231.5 1.6 fusion.47
  233.1 1.6 fusion.46
  234.6 1.6 fusion.45
  236.2 1.6 fusion.44
  237.7 1.6 fusion.43
  239.3 1.6 fusion.42
  240.8 1.6 fusion.41
  242.4 0.7 fusion.40
  243.0 0.7 fusion.39
  243.7 0.7 fusion.38
  244.3 0.7 fusion.37
  245.0 0.7 fusion.36
  245.7 0.7 fusion.35
  246.3 0.7 fusion.34
  247.0 0.7 fusion.33
  247.6 3.7 %all-to-all-start.4 = ((bf16[16,2,1,56,512]{4,3,1,2,0:T(8,128)(2,1)}), bf16[16,2,1,56,512]{4,3,1,2,0:T(8,128)(2,1)S(1)}, u32[]{:S(2)}, u32[]{:S(2)}) async-start(bf16[16,2,1,56,512]{4,3,1,2,0:T(8,128)(2,1)} %fusion.33), calls=%async_computation.5 | async-start | bytes 3670016 | tf_op jit(solution)/shard_map/all_to_all | solution.py:35
  251.4 0.9 slice.57
  252.5 6.3 %fusion.15 = f32[1,768,512]{2,1,0:T(8,128)S(1)} fusion(bf16[768,3712]{1,0:T(8,128)(2,1)} %bitcast.272, bf16[2,3584,512]{2,1,0:T(8,128)(2,1)} %bitcast.276), kind=kOutput, calls=%fused_computation.28 | convolution fusion | flops 2919235584 | bytes 14614528 | tf_op jit(solution)/shard_map/dot_general | solution.py:110
  258.9 1.1 copy-done.9
  260.0 3.1 fusion.18
  263.6 1.5 collective-permute-start
  265.1 32.5 %all-to-all-done.4 = bf16[16,2,1,56,512]{4,3,1,2,0:T(8,128)(2,1)S(1)} async-done(((bf16[16,2,1,56,512]{4,3,1,2,0:T(8,128)(2,1)}), bf16[16,2,1,56,512]{4,3,1,2,0:T(8,128)(2,1)S(1)}, u32[]{:S(2)}, u32[]{:S(2)}) %all-to-all-start.4) | async-done | bytes 1835040 | tf_op jit(solution)/shard_map/all_to_all | solution.py:35
  297.8 1.5 convert.5
  299.3 1.5 convert.6
  300.7 1.3 fusion.27
  302.1 1.0 copy.47
  303.0 0.9 copy.84
  (70 shorter events, 11.7 us)
Async XLA Ops:
  7.2 1.2 copy-start
  7.2 88.9 %reduce-scatter.2.cloned.1.call-start = ((), (), s32[]{:S(2)}) async-start(), calls=%async_computation.6 | async-start | bytes 4587520 | tf_op jit(solution)/shard_map/reduce_scatter | solution.py:88
  12.2 0.7 copy-start.10
  12.2 1.4 copy-start.8
  12.2 1.9 copy-start.11
  12.2 2.3 copy-start.5
  15.6 80.5 %copy-start.6 = (bf16[1,896,512]{2,1,0:T(8,128)(2,1)S(1)}, bf16[1,896,512]{2,1,0:T(8,128)(2,1)}, u32[]{:S(2)}) copy-start(bf16[1,896,512]{2,1,0:T(8,128)(2,1)} %param.15) | copy-start | bytes 2752516
  101.2 3.9 %copy-start.1 = (s32[16]{0:T(128)S(1)}, s32[16]{0:T(128)}, u32[]{:S(2)}) copy-start(s32[16]{0:T(128)} %param.22) | copy-start | bytes 196
  101.2 29.1 %all-to-all-start.1 = ((bf16[1,16,56,512]{3,2,0,1:T(8,128)(2,1)}), bf16[1,16,56,512]{3,2,0,1:T(8,128)(2,1)S(1)}, u32[]{:S(2)}, u32[]{:S(2)}) async-start(bf16[1,16,56,512]{3,2,0,1:T(8,128)(2,1)} %bitcast.266), calls=%async_computation.2 | async-start | bytes 1835008 | tf_op jit(solution)/shard_map/all_to_all | solution.py:32
  105.0 146.4 %all-gather.6.cloned.1.call-start = ((), (), s32[]{:S(2)}) async-start(), calls=%async_computation.8 | async-start | bytes 8552448 | tf_op jit(solution)/shard_map/all_gather | solution.py:98
  143.3 31.0 %all-to-all-start.2 = ((bf16[16,1,1,56,512]{4,3,2,1,0:T(8,128)(2,1)}), bf16[16,1,1,56,512]{4,3,2,1,0:T(8,128)(2,1)S(1)}, u32[]{:S(2)}, u32[]{:S(2)}) async-start(bf16[16,1,1,56,512]{4,3,2,1,0:T(8,128)(2,1)} %constant_dynamic-update-slice_fusion), calls=%async_computation.3 | async-start | bytes 1835008 | tf_op jit(solution)/shard_map/all_to_all | solution.py:35
  147.1 105.4 %all-gather.4.cloned.1.call-start = ((), (), s32[]{:S(2)}) async-start(), calls=%async_computation.7 | async-start | bytes 8257536 | tf_op jit(solution)/shard_map/all_gather | solution.py:106
  174.3 0.9 copy-start.2
  178.2 49.8 %all-to-all-start.3 = ((bf16[2,16,56,512]{3,2,0,1:T(8,128)(2,1)}), bf16[2,16,56,512]{3,2,0,1:T(8,128)(2,1)S(1)}, u32[]{:S(2)}, u32[]{:S(2)}) async-start(bf16[2,16,56,512]{3,2,0,1:T(8,128)(2,1)} %copy.48), calls=%async_computation.4 | async-start | bytes 3670016 | tf_op jit(solution)/shard_map/all_to_all | solution.py:32
  229.8 12.6 %copy-start.4 = (bf16[16,2,56,512]{3,2,1,0:T(8,128)(2,1)S(1)}, bf16[16,2,56,512]{3,2,1,0:T(8,128)(2,1)}, u32[]{:S(2)}) copy-start(bf16[16,2,56,512]{3,2,1,0:T(8,128)(2,1)} %gather_fusion.2) | copy-start | bytes 5505028
  247.6 50.0 %all-to-all-start.4 = ((bf16[16,2,1,56,512]{4,3,1,2,0:T(8,128)(2,1)}), bf16[16,2,1,56,512]{4,3,1,2,0:T(8,128)(2,1)S(1)}, u32[]{:S(2)}, u32[]{:S(2)}) async-start(bf16[16,2,1,56,512]{4,3,1,2,0:T(8,128)(2,1)} %fusion.33), calls=%async_computation.5 | async-start | bytes 3670016 | tf_op jit(solution)/shard_map/all_to_all | solution.py:35
  252.5 6.3 %copy-start.7 = (bf16[32,24,3712]{2,1,0:T(8,128)(2,1)S(1)}, bf16[32,24,3712]{2,1,0:T(8,128)(2,1)}, u32[]{:S(2)}) copy-start(bf16[32,24,3712]{2,1,0:T(8,128)(2,1)} %all-gather.6.cloned.1.call-done) | copy-start | bytes 17104900
  252.5 7.5 %copy-start.9 = (bf16[7168,512]{1,0:T(8,128)(2,1)S(1)}, bf16[7168,512]{1,0:T(8,128)(2,1)}, u32[]{:S(2)}) copy-start(bf16[7168,512]{1,0:T(8,128)(2,1)} %all-gather.4.cloned.1.call-done) | copy-start | bytes 22020100
  263.6 37.1 %collective-permute-start = (bf16[768,256]{1,0:T(8,128)(2,1)S(1)}, bf16[768,256]{1,0:T(8,128)(2,1)}, u32[]{:S(2)}, u32[]{:S(2)}) collective-permute-start(bf16[768,256]{1,0:T(8,128)(2,1)S(1)} %get-tuple-element.30), channel_id=1, source_target_pairs={{0,1},{1,0},{2,3},{3,2},{4,5},{5,4},{6,7},{7,6},{8,9},{9,8},{10,11... | collective-permute-start | bytes 1179656 | tf_op jit(solution)/shard_map/ppermute | solution.py:121
  300.7 2.3 copy-start.3
Sparse Core Ops, SparseCore 0:
  12.3 45.8 reduce-scatter.1
  107.6 94.5 all-gather.5
  204.6 46.3 all-gather.3
